TPU v7x, 512 devices: a whole 4x8x8 slice. The times are simulated.
512 devices in a mesh: row: 16 (over y, x_lo), col: 16 (over z, core), ka: 2 (over x_hi).
Axes of the slice: x: 4 (x_hi: 2, x_lo: 2; x = x_hi * 2 + x_lo), y: 8, z: 8, core: 2. Of those that a mesh axis runs over, the one named last changes fastest.
Arguments:
- pair: bfloat16 [512, 512, 128], P('row', ('col', 'ka')), may hold values from -6 to 6
- pair_mask: int32 [512, 512], P('row', ('col', 'ka')), may hold values from 0 to 1, as said below
- w_in: bfloat16 [2, 128, 512], replicated, may hold values from -0.5 to 0.5
- w_gate: bfloat16 [2, 128, 128], replicated, may hold values from -0.5 to 0.5
- w_out: bfloat16 [2, 128, 128], replicated, may hold values from -0.5 to 0.5
Outputs:
- updated: bfloat16 [512, 512, 128], P('row', ('col', 'ka'))
Inputs may be any that keep to these rules, and one draw needn't show every extreme that they name: pair_mask[i, j] = v[i] v[j] for a per-token 0/1 validity v; within each aligned run of 16 tokens the real tokens come first and there is at least one.
All inputs are finite; a program needn't handle non-finite values.
Results may differ from a plain program's by a relative error of at most 0.014.
Values may be sent and summed in bfloat16 or wider, within the bound.
No kernel may reach another device: no remote copies, remote signals or barrier semaphores. Data moves between devices by JAX's collectives and lax.ppermute only.
A program may use at most 64 MiB of HBM per device.

v0:
```python
import jax
import jax.numpy as jnp
from jax import lax
from jax.sharding import PartitionSpec as P


def layer_norm(value):
    mean = jnp.mean(value, axis=-1, keepdims=True)
    centred = value - mean
    var = jnp.mean(centred * centred, axis=-1, keepdims=True)
    return centred / jnp.sqrt(var + 1e-05)


def prepare(pair, valid, weight_in, weight_gate):
    normed = layer_norm(pair.astype(jnp.float32)).astype(jnp.bfloat16)
    proj = jnp.einsum("ijc,cd->ijd", normed, weight_in, preferred_element_type=jnp.float32)
    width = proj.shape[-1] // 4
    left = (jax.nn.sigmoid(proj[..., :width]) * proj[..., width : 2 * width] * valid).astype(
        jnp.bfloat16
    )
    right = (
        jax.nn.sigmoid(proj[..., 2 * width : 3 * width]) * proj[..., 3 * width :] * valid
    ).astype(jnp.bfloat16)
    gate = jax.nn.sigmoid(
        jnp.einsum("ijc,cd->ijd", normed, weight_gate, preferred_element_type=jnp.float32)
    )
    return (left, right, gate)


def finish(pair, tri, gate, weight_out):
    normed = layer_norm(tri).astype(jnp.bfloat16)
    proj = jnp.einsum("ijc,cd->ijd", normed, weight_out, preferred_element_type=jnp.float32)
    return (pair.astype(jnp.float32) + gate * proj).astype(jnp.bfloat16)


def transpose_tiles(value, n):
    perm = [(r * n + c, c * n + r) for r in range(n) for c in range(n)]
    return lax.ppermute(value, ("row", "col"), perm)


def gather_a2a(value, axis_name, n, axis):
    copies = jnp.broadcast_to(value[None], (n,) + value.shape)
    got = lax.all_to_all(copies, axis_name, 0, 0, tiled=False)
    got = jnp.moveaxis(got, 0, axis)
    return got.reshape(value.shape[:axis] + (n * value.shape[axis],) + value.shape[axis + 1 :])


def sum_over_ka(partial_value):
    half = partial_value.shape[1] // 2
    me = lax.axis_index("ka")
    mine = lax.dynamic_slice_in_dim(partial_value, me * half, half, axis=1)
    theirs = lax.dynamic_slice_in_dim(partial_value, (1 - me) * half, half, axis=1)
    got = lax.ppermute(theirs.astype(jnp.bfloat16), "ka", [(0, 1), (1, 0)])
    return mine + got.astype(jnp.float32)


def join_over_ka(value):
    me = lax.axis_index("ka")
    got = lax.ppermute(value, "ka", [(0, 1), (1, 0)])
    return jnp.where(
        me == 0, jnp.concatenate([value, got], axis=1), jnp.concatenate([got, value], axis=1)
    )


def on_device(n, pair, pair_mask, w_in, w_gate, w_out):
    valid = pair_mask.astype(jnp.float32)[..., None]
    left, right, gate = prepare(pair, valid, w_in[0], w_gate[0])
    left_rows = lax.all_gather(jnp.swapaxes(left, 0, 1), "col", axis=0, tiled=True)
    right_diag = gather_a2a(jnp.swapaxes(transpose_tiles(right, n), 0, 1), "row", n, 0)
    half = right_diag.shape[1] // 2
    me = lax.axis_index("ka")
    theirs = lax.dynamic_slice_in_dim(right_diag, (1 - me) * half, half, axis=1)
    mine = lax.dynamic_slice_in_dim(right_diag, me * half, half, axis=1)
    sent = jnp.sum(
        left_rows[:, :, None].astype(jnp.float32) * theirs[:, None].astype(jnp.float32), axis=0
    ).astype(jnp.bfloat16)
    sent, left_later, mine = lax.optimization_barrier((sent, left_rows, mine))
    got = lax.ppermute(sent, "ka", [(0, 1), (1, 0)])
    kept = jnp.sum(
        left_later[:, :, None].astype(jnp.float32) * mine[:, None].astype(jnp.float32), axis=0
    )
    tri = kept + got.astype(jnp.float32)
    middle = finish(pair, tri, gate, w_out[0])
    left, right, gate = prepare(middle, valid, w_in[1], w_gate[1])
    right_cols = gather_a2a(right, "row", n, 0)
    left_tile = join_over_ka(transpose_tiles(left, n))
    left_diag = lax.all_gather(left_tile, "col", axis=0, tiled=True)
    tri = jnp.sum(left_diag[:, :, None] * right_cols[:, None], axis=0, dtype=jnp.float32)
    return finish(middle, tri, gate, w_out[1])


def solution(mesh):
    n = mesh.shape["row"]
    assert mesh.shape["col"] == n
    placed = (P("row", ("col", "ka"), None), P("row", ("col", "ka")), P(), P(), P())
    return jax.shard_map(
        lambda *a: on_device(n, *a),
        mesh=mesh,
        in_specs=placed,
        out_specs=P("row", ("col", "ka"), None),
        check_vma=False,
    )
```

profile of v0, /device:TPU:4, one launch (start us, length us, event | category | flops | bytes accessed | tf_op | source)
XLA Modules:
  0.0 218.7 jit_solution(2915067116465360204)
XLA Ops:
  6.5 0.0 all-gather.3.cloned.1.call-start
  6.5 1.0 convert_reduce_fusion.2
  7.6 1.1 fusion.13
  8.8 0.7 convert_element_type.68
  9.5 0.1 copy.14
  9.5 1.3 fusion.37
  10.9 0.0 copy-start.2
  10.9 0.0 copy-start.4
  10.9 0.8 fusion.45
  11.7 0.7 collective-permute-start
  12.4 0.0 all-gather.3.cloned.1.call-update
  12.4 0.0 collective-permute-done
  12.5 1.8 broadcast_in_dim.4
  14.2 26.5 %all-to-all-start = ((bf16[16,16,32,128]{3,2,1,0:T(8,128)(2,1)}), bf16[16,16,32,128]{3,2,1,0:T(8,128)(2,1)S(1)}, u32[]{:S(2)}, u32[]{:S(2)}) async-start(bf16[16,16,32,128]{3,2,1,0:T(8,128)(2,1)} %broadcast_in_dim.4), calls=%async_computation | async-start | bytes 4194304 | tf_op jit(solution)/shard_map/all_to_all | solution.py:43
  40.8 0.0 all-gather.5.cloned.1.call-start
  40.8 0.0 copy-done.2
  40.8 0.0 copy-done.4
  40.8 0.3 fusion.7
  41.2 24.9 %all-gather.3.cloned.1.call-done = bf16[256,32,128]{2,0,1:T(8,128)(2,1)} async-done(((bf16[16,32,128]{2,0,1:T(8,128)(2,1)}), bf16[256,32,128]{2,0,1:T(8,128)(2,1)}) %all-gather.3.cloned.1.call-update) | async-done | bytes 2097168 | tf_op jit(solution)/shard_map/all_gather | solution.py:68
  66.1 4.7 %copy.15 = f32[256,32,128]{2,1,0:T(8,128)} copy(bf16[256,32,128]{2,0,1:T(8,128)(2,1)} %all-gather.3.cloned.1.call-done) | data formatting | bytes 6291456 | tf_op jit(solution)/shard_map/convert_element_type | solution.py:75
  70.8 20.6 %all-to-all-done = bf16[16,16,32,128]{3,2,1,0:T(8,128)(2,1)S(1)} async-done(((bf16[16,16,32,128]{3,2,1,0:T(8,128)(2,1)}), bf16[16,16,32,128]{3,2,1,0:T(8,128)(2,1)S(1)}, u32[]{:S(2)}, u32[]{:S(2)}) %all-to-all-start) | async-done | bytes 2097184 | tf_op jit(solution)/shard_map/all_to_all | solution.py:43
  91.4 0.0 copy-start
  91.4 0.3 constant_dynamic-slice_fusion
  91.7 0.0 copy-start.1
  91.7 1.9 copy-done
  93.6 5.6 %multiply_reduce_fusion.1 = bf16[32,16,128]{2,1,0:T(8,128)(2,1)S(1)} fusion(f32[256,16,128]{2,1,0:T(8,128)S(1)} %get-tuple-element.14, f32[256,32,128]{2,1,0:T(8,128)S(1)} %copy-done), kind=kLoop, calls=%fused_computation.3 | loop fusion | flops 33488896 | bytes 6422528 | tf_op jit(solution)/shard_map/reduce_sum | solution.py:74
  99.2 0.0 copy-done.1
  99.2 1.2 copy.17
  100.5 0.2 convert_element_type.75
  100.6 0.0 copy-start.5
  100.6 0.0 copy-start.3
  100.6 3.0 %collective-permute-start.1 = (bf16[32,16,128]{2,1,0:T(8,128)(2,1)S(1)}, bf16[32,16,128]{2,1,0:T(8,128)(2,1)S(1)}, u32[]{:S(2)}, u32[]{:S(2)}) collective-permute-start(bf16[32,16,128]{2,1,0:T(8,128)(2,1)S(1)} %multiply_reduce_fusion.1), channel_id=1, source_target_pairs={{0,1},{1,0},{2,3},{3,2},{4,5},{5,4},{6,7},{7,6},{8,9},{9,8},{10,11... | collective-permute-start | bytes 393224 | tf_op jit(solution)/shard_map/ppermute | solution.py:78
  103.6 5.6 %multiply_reduce_fusion = f32[32,16,128]{2,1,0:T(8,128)S(1)} fusion(f32[256,16,128]{2,1,0:T(8,128)S(1)} %convert_element_type.75, f32[256,32,128]{2,1,0:T(8,128)S(1)} %copy.17), kind=kLoop, calls=%fused_computation.2 | loop fusion | flops 33488896 | bytes 6553600 | tf_op jit(solution)/shard_map/reduce_sum | solution.py:79
  109.3 0.0 collective-permute-done.1
  109.3 0.1 fusion.46
  109.4 0.2 multiply_reduce_fusion.4
  109.7 0.0 copy-done.5
  109.7 0.4 fusion.57
  110.1 0.2 multiply_reduce_fusion.3
  110.4 0.0 copy-done.3
  110.4 0.4 fusion.35
  110.8 0.2 fusion.21
  110.9 0.7 collective-permute-start.2
  111.6 0.0 collective-permute-done.2
  111.6 4.5 %collective-permute-start.3 = (bf16[32,16,128]{2,1,0:T(8,128)(2,1)S(1)}, bf16[32,16,128]{2,1,0:T(8,128)(2,1)S(1)}, u32[]{:S(2)}, u32[]{:S(2)}) collective-permute-start(bf16[32,16,128]{2,1,0:T(8,128)(2,1)S(1)} %collective-permute-done.2), channel_id=1, source_target_pairs={{0,1},{1,0},{2,3},{3,2},{4,5},{5,4},{6,7},{7,6},{8,9},{9,8},{10,11... | collective-permute-start | bytes 393224 | tf_op jit(solution)/shard_map/ppermute | solution.py:59
  116.1 3.8 %collective-permute-done.3 = bf16[32,16,128]{2,1,0:T(8,128)(2,1)S(1)} collective-permute-done((bf16[32,16,128]{2,1,0:T(8,128)(2,1)S(1)}, bf16[32,16,128]{2,1,0:T(8,128)(2,1)S(1)}, u32[]{:S(2)}, u32[]{:S(2)}) %collective-permute-start.3) | collective-permute-done | bytes 131104 | tf_op jit(solution)/shard_map/ppermute | solution.py:59
  120.0 0.8 maximum_select_fusion
  120.8 0.0 all-gather.5.cloned.1.call-update
  120.8 1.7 broadcast_in_dim.5
  122.6 23.4 %all-to-all-start.1 = ((bf16[16,32,16,128]{3,2,1,0:T(8,128)(2,1)}), bf16[16,32,16,128]{3,2,1,0:T(8,128)(2,1)S(1)}, u32[]{:S(2)}, u32[]{:S(2)}) async-start(bf16[16,32,16,128]{3,2,1,0:T(8,128)(2,1)} %broadcast_in_dim.5), calls=%async_computation.1 | async-start | bytes 4194304 | tf_op jit(solution)/shard_map/all_to_all | solution.py:43
  146.0 0.3 fusion.4
  146.3 48.9 %all-to-all-done.1 = bf16[16,32,16,128]{3,2,1,0:T(8,128)(2,1)S(1)} async-done(((bf16[16,32,16,128]{3,2,1,0:T(8,128)(2,1)}), bf16[16,32,16,128]{3,2,1,0:T(8,128)(2,1)S(1)}, u32[]{:S(2)}, u32[]{:S(2)}) %all-to-all-start.1) | async-done | bytes 2097184 | tf_op jit(solution)/shard_map/all_to_all | solution.py:43
  195.2 0.0 all-gather.5.cloned.1.call-done
  195.2 15.3 %convert_reduce_fusion = (f32[32,16]{1,0:T(8,128)S(1)}, f32[32,16,128]{2,1,0:T(8,128)S(1)}) fusion(bf16[512,16,128]{2,1,0:T(8,128)(2,1)S(1)} %bitcast.31, bf16[512,32,128]{2,1,0:T(8,128)(2,1)} %all-gather.5.cloned.1.call-done), kind=kLoop, calls=%fused_computation | loop fusion | flops 134151680 | bytes 6555648 | tf_op jit(solution)/shard_map/reduce_sum | solution.py:8
  210.6 0.2 multiply_reduce_fusion.2
  210.8 1.0 fusion.10
  (9 shorter events, 0.1 us)
Async XLA Ops:
  6.5 59.5 %all-gather.3.cloned.1.call-start = ((), (), s32[]{:S(2)}) async-start(), calls=%async_computation.2 | async-start | bytes 2228224 | tf_op jit(solution)/shard_map/all_gather | solution.py:68
  10.9 29.9 %copy-start.2 = (bf16[32,16,128]{2,1,0:T(8,128)(2,1)S(1)}, bf16[32,16,128]{2,1,0:T(8,128)(2,1)}, u32[]{:S(2)}) copy-start(bf16[32,16,128]{2,1,0:T(8,128)(2,1)} %param.5) | copy-start | bytes 393220
  10.9 29.9 %copy-start.4 = (bf16[2,128,128]{2,1,0:T(8,128)(2,1)S(1)}, bf16[2,128,128]{2,1,0:T(8,128)(2,1)}, u32[]{:S(2)}) copy-start(bf16[2,128,128]{2,1,0:T(8,128)(2,1)} %param.8) | copy-start | bytes 196612
  11.7 0.7 collective-permute-start
  14.2 77.2 %all-to-all-start = ((bf16[16,16,32,128]{3,2,1,0:T(8,128)(2,1)}), bf16[16,16,32,128]{3,2,1,0:T(8,128)(2,1)S(1)}, u32[]{:S(2)}, u32[]{:S(2)}) async-start(bf16[16,16,32,128]{3,2,1,0:T(8,128)(2,1)} %broadcast_in_dim.4), calls=%async_computation | async-start | bytes 4194304 | tf_op jit(solution)/shard_map/all_to_all | solution.py:43
  40.8 154.5 %all-gather.5.cloned.1.call-start = ((), (), s32[]{:S(2)}) async-start(), calls=%async_computation.3 | async-start | bytes 4456448 | tf_op jit(solution)/shard_map/all_gather | solution.py:87
  91.4 2.2 %copy-start = (f32[256,32,128]{2,1,0:T(8,128)S(1)}, f32[256,32,128]{2,1,0:T(8,128)}, u32[]{:S(2)}) copy-start(f32[256,32,128]{2,1,0:T(8,128)} %copy.15) | copy-start | bytes 12582916
  91.7 7.5 %copy-start.1 = (bf16[256,32,128]{2,0,1:T(8,128)(2,1)S(1)}, bf16[256,32,128]{2,0,1:T(8,128)(2,1)}, u32[]{:S(2)}) copy-start(bf16[256,32,128]{2,0,1:T(8,128)(2,1)} %all-gather.3.cloned.1.call-done) | copy-start | bytes 6291460
  100.6 9.1 %copy-start.5 = (bf16[2,128,128]{2,1,0:T(8,128)(2,1)S(1)}, bf16[2,128,128]{2,1,0:T(8,128)(2,1)}, u32[]{:S(2)}) copy-start(bf16[2,128,128]{2,1,0:T(8,128)(2,1)} %param.9) | copy-start | bytes 196612
  100.6 9.8 %copy-start.3 = (bf16[2,128,512]{2,1,0:T(8,128)(2,1)S(1)}, bf16[2,128,512]{2,1,0:T(8,128)(2,1)}, u32[]{:S(2)}) copy-start(bf16[2,128,512]{2,1,0:T(8,128)(2,1)} %param.7) | copy-start | bytes 786436
  100.6 8.6 %collective-permute-start.1 = (bf16[32,16,128]{2,1,0:T(8,128)(2,1)S(1)}, bf16[32,16,128]{2,1,0:T(8,128)(2,1)S(1)}, u32[]{:S(2)}, u32[]{:S(2)}) collective-permute-start(bf16[32,16,128]{2,1,0:T(8,128)(2,1)S(1)} %multiply_reduce_fusion.1), channel_id=1, source_target_pairs={{0,1},{1,0},{2,3},{3,2},{4,5},{5,4},{6,7},{7,6},{8,9},{9,8},{10,11... | collective-permute-start | bytes 393224 | tf_op jit(solution)/shard_map/ppermute | solution.py:78
  110.9 0.7 collective-permute-start.2
  111.6 8.4 %collective-permute-start.3 = (bf16[32,16,128]{2,1,0:T(8,128)(2,1)S(1)}, bf16[32,16,128]{2,1,0:T(8,128)(2,1)S(1)}, u32[]{:S(2)}, u32[]{:S(2)}) collective-permute-start(bf16[32,16,128]{2,1,0:T(8,128)(2,1)S(1)} %collective-permute-done.2), channel_id=1, source_target_pairs={{0,1},{1,0},{2,3},{3,2},{4,5},{5,4},{6,7},{7,6},{8,9},{9,8},{10,11... | collective-permute-start | bytes 393224 | tf_op jit(solution)/shard_map/ppermute | solution.py:59
  122.6 72.6 %all-to-all-start.1 = ((bf16[16,32,16,128]{3,2,1,0:T(8,128)(2,1)}), bf16[16,32,16,128]{3,2,1,0:T(8,128)(2,1)S(1)}, u32[]{:S(2)}, u32[]{:S(2)}) async-start(bf16[16,32,16,128]{3,2,1,0:T(8,128)(2,1)} %broadcast_in_dim.5), calls=%async_computation.1 | async-start | bytes 4194304 | tf_op jit(solution)/shard_map/all_to_all | solution.py:43
Sparse Core Ops, SparseCore 0:
  12.5 53.4 all-gather.2
  121.0 62.3 all-gather.4
where the time goes:
time: 219 us
  waiting for transfers between devices  98.3 us (45%)
  starting transfers between devices  58.8 us (27%)
  other arithmetic  32.7 us (15%)
  between operations  13.8 us (6%)
  local copies, waits for them, and re-layouts  11.5 us (5%)
  matrix products  3.73 us (2%)
    all_to_all x2, waiting for transfers between devices, gather_a2a(): got = lax.all_to_all(copies, axis_name, 0, 0, tiled=False)  69.5 us
    all_to_all x2, starting transfers between devices, gather_a2a(): got = lax.all_to_all(copies, axis_name, 0, 0, tiled=False)  49.9 us
    all_gather x1, waiting for transfers between devices, on_device(): lax.all_gather(jnp.swapaxes(left, 0, 1), 'col', axis=0, tiled=True)  24.9 us
    reduce_sum x3, other arithmetic, layer_norm(): mean = jnp.mean(value, axis=-1, keepdims=True)  16.5 us
    reduce_sum x1, other arithmetic, on_device(): jnp.sum(left_rows[:, :, None].astype(jnp.float32) * theirs[:, None].astyp...  5.63 us
    reduce_sum x1, other arithmetic, on_device(): jnp.sum(left_later[:, :, None].astype(jnp.float32) * mine[:, None].astype...  5.62 us
    convert_element_type x1, local copies, waits for them, and re-layouts, on_device(): left_rows[:, :, None].astype(jnp.float32)  4.73 us
    ppermute x1, starting transfers between devices, join_over_ka(): got = lax.ppermute(value, 'ka', [(0, 1), (1, 0)])  4.5 us
  transfers between devices with their start and end apart: 8, of which 4 were waited for; matrix products, arithmetic and copies ran while one was open for 7% of the time, Pallas kernels for 0%

commit v1 on v0

--- a/solution.py
+++ b/solution.py
@@ -65,7 +65,10 @@
 def on_device(n, pair, pair_mask, w_in, w_gate, w_out):
     valid = pair_mask.astype(jnp.float32)[..., None]
     left, right, gate = prepare(pair, valid, w_in[0], w_gate[0])
-    left_rows = lax.all_gather(jnp.swapaxes(left, 0, 1), "col", axis=0, tiled=True)
+    left_rows = jnp.concatenate(
+        lax.all_to_all(jnp.stack([jnp.swapaxes(left, 0, 1)] * lax.axis_size("col")), "col", 0, 0),
+        axis=0,
+    )
     right_diag = gather_a2a(jnp.swapaxes(transpose_tiles(right, n), 0, 1), "row", n, 0)
     half = right_diag.shape[1] // 2
     me = lax.axis_index("ka")

time: 219 us -> 270 us (1.23)
  the two profiles are of different devices: /device:TPU:4 before, /device:TPU:1 now
where the time goes in v1:
time: 270 us; the launch traced here: 269 us
  waiting for transfers between devices  159 us (59%)
  starting transfers between devices  49.9 us (18%)
  other arithmetic  36.9 us (14%)
  between operations  13.7 us (5%)
  local copies, waits for them, and re-layouts  6.27 us (2%)
  matrix products  3.72 us (1%)
    all_to_all x2, waiting for transfers between devices, gather_a2a(): got = lax.all_to_all(copies, axis_name, 0, 0, tiled=False)  95.8 us
    all_to_all x1, waiting for transfers between devices, on_device(): lax.all_to_all(jnp.stack([jnp.swapaxes(left, 0, 1)] * lax.axis_size('col'...  50.1 us
    all_to_all x2, starting transfers between devices, gather_a2a(): got = lax.all_to_all(copies, axis_name, 0, 0, tiled=False)  25.2 us
    reduce_sum x3, other arithmetic, layer_norm(): mean = jnp.mean(value, axis=-1, keepdims=True)  16.5 us
    all_to_all x1, starting transfers between devices, on_device(): lax.all_to_all(jnp.stack([jnp.swapaxes(left, 0, 1)] * lax.axis_size('col'...  11.8 us
    ppermute x2, waiting for transfers between devices, transpose_tiles(): return lax.ppermute(value, ('row', 'col'), perm)  7.89 us
    ppermute x2, starting transfers between devices, transpose_tiles(): return lax.ppermute(value, ('row', 'col'), perm)  6.28 us
    reduce_sum x1, other arithmetic, on_device(): jnp.sum(left_rows[:, :, None].astype(jnp.float32) * theirs[:, None].astyp...  5.63 us
  transfers between devices with their start and end apart: 8, of which 6 were waited for; matrix products, arithmetic and copies ran while one was open for 4% of the time, Pallas kernels for 0%

profile of v1, /device:TPU:1, one launch (start us, length us, event | category | flops | bytes accessed | tf_op | source)
XLA Modules:
  0.0 269.4 jit_solution(12537263196203160141)
XLA Ops:
  6.5 1.0 convert_reduce_fusion.2
  7.6 1.1 fusion.13
  8.8 0.7 convert_element_type.72
  9.5 0.1 copy.12
  9.5 1.3 fusion.37
  10.9 0.2 fusion.45
  11.1 1.8 stack.2
  12.8 11.8 %all-to-all-start = ((bf16[16,16,32,128]{3,2,1,0:T(8,128)(2,1)}), bf16[16,16,32,128]{3,2,1,0:T(8,128)(2,1)S(1)}, u32[]{:S(2)}, u32[]{:S(2)}) async-start(bf16[16,16,32,128]{3,2,1,0:T(8,128)(2,1)} %stack.2), calls=%async_computation | async-start | bytes 4194304 | tf_op jit(solution)/shard_map/all_to_all | solution.py:69
  24.7 0.0 copy-start.1
  24.7 0.0 copy-start.3
  24.7 3.3 %collective-permute-start = (bf16[32,16,128]{2,1,0:T(8,128)(2,1)S(1)}, bf16[32,16,128]{2,1,0:T(8,128)(2,1)S(1)}, u32[]{:S(2)}, u32[]{:S(2)}) collective-permute-start(bf16[32,16,128]{2,1,0:T(8,128)(2,1)S(1)} %get-tuple-element.18), channel_id=1, source_target_pairs={{0,0},{2,32},{4,64},{6,96},{8,128},{10,160},{12,192},{14,224},{16,... | collective-permute-start | bytes 393224 | tf_op jit(solution)/shard_map/ppermute | solution.py:38
  27.9 3.5 %collective-permute-done = bf16[32,16,128]{2,1,0:T(8,128)(2,1)S(1)} collective-permute-done((bf16[32,16,128]{2,1,0:T(8,128)(2,1)S(1)}, bf16[32,16,128]{2,1,0:T(8,128)(2,1)S(1)}, u32[]{:S(2)}, u32[]{:S(2)}) %collective-permute-start) | collective-permute-done | bytes 131104 | tf_op jit(solution)/shard_map/ppermute | solution.py:38
  31.4 50.1 %all-to-all-done = bf16[16,16,32,128]{3,2,1,0:T(8,128)(2,1)S(1)} async-done(((bf16[16,16,32,128]{3,2,1,0:T(8,128)(2,1)}), bf16[16,16,32,128]{3,2,1,0:T(8,128)(2,1)S(1)}, u32[]{:S(2)}, u32[]{:S(2)}) %all-to-all-start) | async-done | bytes 2097184 | tf_op jit(solution)/shard_map/all_to_all | solution.py:69
  81.6 1.7 broadcast_in_dim.4
  83.3 11.4 %all-to-all-start.1 = ((bf16[16,16,32,128]{3,2,1,0:T(8,128)(2,1)}), bf16[16,16,32,128]{3,2,1,0:T(8,128)(2,1)}, u32[]{:S(2)}, u32[]{:S(2)}) async-start(bf16[16,16,32,128]{3,2,1,0:T(8,128)(2,1)} %broadcast_in_dim.4), calls=%async_computation.1 | async-start | bytes 4194304 | tf_op jit(solution)/shard_map/all_to_all | solution.py:43
  94.7 0.0 all-gather.2.cloned.1.call-start
  94.8 0.0 copy-done.1
  94.8 0.0 copy-done.3
  94.8 0.3 fusion.7
  95.1 2.7 bitcast_convert_fusion
  97.8 47.2 %all-to-all-done.1 = bf16[16,16,32,128]{3,2,1,0:T(8,128)(2,1)} async-done(((bf16[16,16,32,128]{3,2,1,0:T(8,128)(2,1)}), bf16[16,16,32,128]{3,2,1,0:T(8,128)(2,1)}, u32[]{:S(2)}, u32[]{:S(2)}) %all-to-all-start.1) | async-done | bytes 2097184 | tf_op jit(solution)/shard_map/all_to_all | solution.py:43
  145.0 0.0 copy-start
  145.0 2.0 constant_dynamic-slice_fusion
  147.0 0.9 copy-done
  147.9 5.6 %multiply_reduce_fusion.1 = bf16[32,16,128]{2,1,0:T(8,128)(2,1)S(1)} fusion(f32[256,16,128]{2,1,0:T(8,128)S(1)} %get-tuple-element.14, f32[256,32,128]{2,1,0:T(8,128)S(1)} %copy-done), kind=kLoop, calls=%fused_computation.3 | loop fusion | flops 33488896 | bytes 6422528 | tf_op jit(solution)/shard_map/reduce_sum | solution.py:77
  153.5 0.6 convert_element_type.78
  154.1 0.2 convert_element_type.79
  154.2 0.0 copy-start.4
  154.3 0.0 copy-start.2
  154.3 4.5 %collective-permute-start.1 = (bf16[32,16,128]{2,1,0:T(8,128)(2,1)S(1)}, bf16[32,16,128]{2,1,0:T(8,128)(2,1)S(1)}, u32[]{:S(2)}, u32[]{:S(2)}) collective-permute-start(bf16[32,16,128]{2,1,0:T(8,128)(2,1)S(1)} %multiply_reduce_fusion.1), channel_id=1, source_target_pairs={{0,1},{1,0},{2,3},{3,2},{4,5},{5,4},{6,7},{7,6},{8,9},{9,8},{10,11... | collective-permute-start | bytes 393224 | tf_op jit(solution)/shard_map/ppermute | solution.py:81
  158.8 5.6 %multiply_reduce_fusion = f32[32,16,128]{2,1,0:T(8,128)S(1)} fusion(f32[256,16,128]{2,1,0:T(8,128)S(1)} %convert_element_type.79, f32[256,32,128]{2,1,0:T(8,128)S(1)} %convert_element_type.78), kind=kLoop, calls=%fused_computation.2 | loop fusion | flops 33488896 | bytes 6553600 | tf_op jit(solution)/shard_map/reduce_sum | solution.py:82
  164.4 0.0 collective-permute-done.1
  164.4 0.1 fusion.46
  164.6 0.2 multiply_reduce_fusion.4
  164.8 0.0 copy-done.4
  164.8 0.4 fusion.57
  165.3 0.2 multiply_reduce_fusion.3
  165.5 0.0 copy-done.2
  165.5 0.4 fusion.35
  165.9 0.2 fusion.21
  166.1 3.0 %collective-permute-start.2 = (bf16[32,16,128]{2,1,0:T(8,128)(2,1)S(1)}, bf16[32,16,128]{2,1,0:T(8,128)(2,1)S(1)}, u32[]{:S(2)}, u32[]{:S(2)}) collective-permute-start(bf16[32,16,128]{2,1,0:T(8,128)(2,1)S(1)} %get-tuple-element.15), channel_id=1, source_target_pairs={{0,0},{2,32},{4,64},{6,96},{8,128},{10,160},{12,192},{14,224},{16,... | collective-permute-start | bytes 393224 | tf_op jit(solution)/shard_map/ppermute | solution.py:38
  169.1 4.4 %collective-permute-done.2 = bf16[32,16,128]{2,1,0:T(8,128)(2,1)S(1)} collective-permute-done((bf16[32,16,128]{2,1,0:T(8,128)(2,1)S(1)}, bf16[32,16,128]{2,1,0:T(8,128)(2,1)S(1)}, u32[]{:S(2)}, u32[]{:S(2)}) %collective-permute-start.2) | collective-permute-done | bytes 131104 | tf_op jit(solution)/shard_map/ppermute | solution.py:38
  173.5 2.1 collective-permute-start.3
  175.7 5.1 %collective-permute-done.3 = bf16[32,16,128]{2,1,0:T(8,128)(2,1)S(1)} collective-permute-done((bf16[32,16,128]{2,1,0:T(8,128)(2,1)S(1)}, bf16[32,16,128]{2,1,0:T(8,128)(2,1)S(1)}, u32[]{:S(2)}, u32[]{:S(2)}) %collective-permute-start.3) | collective-permute-done | bytes 131104 | tf_op jit(solution)/shard_map/ppermute | solution.py:59
  180.7 0.8 maximum_select_fusion
  181.6 0.0 all-gather.2.cloned.1.call-update
  181.6 1.7 broadcast_in_dim.5
  183.3 13.8 %all-to-all-start.2 = ((bf16[16,32,16,128]{3,2,1,0:T(8,128)(2,1)}), bf16[16,32,16,128]{3,2,1,0:T(8,128)(2,1)S(1)}, u32[]{:S(2)}, u32[]{:S(2)}) async-start(bf16[16,32,16,128]{3,2,1,0:T(8,128)(2,1)} %broadcast_in_dim.5), calls=%async_computation.2 | async-start | bytes 4194304 | tf_op jit(solution)/shard_map/all_to_all | solution.py:43
  197.1 0.3 fusion.4
  197.4 48.5 %all-to-all-done.2 = bf16[16,32,16,128]{3,2,1,0:T(8,128)(2,1)S(1)} async-done(((bf16[16,32,16,128]{3,2,1,0:T(8,128)(2,1)}), bf16[16,32,16,128]{3,2,1,0:T(8,128)(2,1)S(1)}, u32[]{:S(2)}, u32[]{:S(2)}) %all-to-all-start.2) | async-done | bytes 2097184 | tf_op jit(solution)/shard_map/all_to_all | solution.py:43
  246.0 0.0 all-gather.2.cloned.1.call-done
  246.0 15.3 %convert_reduce_fusion = (f32[32,16]{1,0:T(8,128)S(1)}, f32[32,16,128]{2,1,0:T(8,128)S(1)}) fusion(bf16[512,16,128]{2,1,0:T(8,128)(2,1)S(1)} %bitcast.34, bf16[512,32,128]{2,1,0:T(8,128)(2,1)} %all-gather.2.cloned.1.call-done), kind=kLoop, calls=%fused_computation | loop fusion | flops 134151680 | bytes 6555648 | tf_op jit(solution)/shard_map/reduce_sum | solution.py:8
  261.3 0.2 multiply_reduce_fusion.2
  261.6 1.0 fusion.10
  (10 shorter events, 0.1 us)
Async XLA Ops:
  12.8 68.7 %all-to-all-start = ((bf16[16,16,32,128]{3,2,1,0:T(8,128)(2,1)}), bf16[16,16,32,128]{3,2,1,0:T(8,128)(2,1)S(1)}, u32[]{:S(2)}, u32[]{:S(2)}) async-start(bf16[16,16,32,128]{3,2,1,0:T(8,128)(2,1)} %stack.2), calls=%async_computation | async-start | bytes 4194304 | tf_op jit(solution)/shard_map/all_to_all | solution.py:69
  24.7 70.1 %copy-start.1 = (bf16[32,16,128]{2,1,0:T(8,128)(2,1)S(1)}, bf16[32,16,128]{2,1,0:T(8,128)(2,1)}, u32[]{:S(2)}) copy-start(bf16[32,16,128]{2,1,0:T(8,128)(2,1)} %param.5) | copy-start | bytes 393220
  24.7 70.1 %copy-start.3 = (bf16[2,128,128]{2,1,0:T(8,128)(2,1)S(1)}, bf16[2,128,128]{2,1,0:T(8,128)(2,1)}, u32[]{:S(2)}) copy-start(bf16[2,128,128]{2,1,0:T(8,128)(2,1)} %param.8) | copy-start | bytes 196612
  24.7 6.7 %collective-permute-start = (bf16[32,16,128]{2,1,0:T(8,128)(2,1)S(1)}, bf16[32,16,128]{2,1,0:T(8,128)(2,1)S(1)}, u32[]{:S(2)}, u32[]{:S(2)}) collective-permute-start(bf16[32,16,128]{2,1,0:T(8,128)(2,1)S(1)} %get-tuple-element.18), channel_id=1, source_target_pairs={{0,0},{2,32},{4,64},{6,96},{8,128},{10,160},{12,192},{14,224},{16,... | collective-permute-start | bytes 393224 | tf_op jit(solution)/shard_map/ppermute | solution.py:38
  83.3 61.7 %all-to-all-start.1 = ((bf16[16,16,32,128]{3,2,1,0:T(8,128)(2,1)}), bf16[16,16,32,128]{3,2,1,0:T(8,128)(2,1)}, u32[]{:S(2)}, u32[]{:S(2)}) async-start(bf16[16,16,32,128]{3,2,1,0:T(8,128)(2,1)} %broadcast_in_dim.4), calls=%async_computation.1 | async-start | bytes 4194304 | tf_op jit(solution)/shard_map/all_to_all | solution.py:43
  94.7 151.2 %all-gather.2.cloned.1.call-start = ((), (), s32[]{:S(2)}) async-start(), calls=%async_computation.3 | async-start | bytes 4456448 | tf_op jit(solution)/shard_map/all_gather | solution.py:90
  145.0 2.8 %copy-start = (f32[256,32,128]{2,1,0:T(8,128)S(1)}, f32[256,32,128]{2,1,0:T(8,128)}, u32[]{:S(2)}) copy-start(f32[256,32,128]{2,1,0:T(8,128)} %bitcast_convert_fusion) | copy-start | bytes 12582916
  154.2 10.6 %copy-start.4 = (bf16[2,128,128]{2,1,0:T(8,128)(2,1)S(1)}, bf16[2,128,128]{2,1,0:T(8,128)(2,1)}, u32[]{:S(2)}) copy-start(bf16[2,128,128]{2,1,0:T(8,128)(2,1)} %param.9) | copy-start | bytes 196612
  154.3 11.3 %copy-start.2 = (bf16[2,128,512]{2,1,0:T(8,128)(2,1)S(1)}, bf16[2,128,512]{2,1,0:T(8,128)(2,1)}, u32[]{:S(2)}) copy-start(bf16[2,128,512]{2,1,0:T(8,128)(2,1)} %param.7) | copy-start | bytes 786436
  154.3 10.1 %collective-permute-start.1 = (bf16[32,16,128]{2,1,0:T(8,128)(2,1)S(1)}, bf16[32,16,128]{2,1,0:T(8,128)(2,1)S(1)}, u32[]{:S(2)}, u32[]{:S(2)}) collective-permute-start(bf16[32,16,128]{2,1,0:T(8,128)(2,1)S(1)} %multiply_reduce_fusion.1), channel_id=1, source_target_pairs={{0,1},{1,0},{2,3},{3,2},{4,5},{5,4},{6,7},{7,6},{8,9},{9,8},{10,11... | collective-permute-start | bytes 393224 | tf_op jit(solution)/shard_map/ppermute | solution.py:81
  166.1 7.5 %collective-permute-start.2 = (bf16[32,16,128]{2,1,0:T(8,128)(2,1)S(1)}, bf16[32,16,128]{2,1,0:T(8,128)(2,1)S(1)}, u32[]{:S(2)}, u32[]{:S(2)}) collective-permute-start(bf16[32,16,128]{2,1,0:T(8,128)(2,1)S(1)} %get-tuple-element.15), channel_id=1, source_target_pairs={{0,0},{2,32},{4,64},{6,96},{8,128},{10,160},{12,192},{14,224},{16,... | collective-permute-start | bytes 393224 | tf_op jit(solution)/shard_map/ppermute | solution.py:38
  173.5 7.2 %collective-permute-start.3 = (bf16[32,16,128]{2,1,0:T(8,128)(2,1)S(1)}, bf16[32,16,128]{2,1,0:T(8,128)(2,1)S(1)}, u32[]{:S(2)}, u32[]{:S(2)}) collective-permute-start(bf16[32,16,128]{2,1,0:T(8,128)(2,1)S(1)} %collective-permute-done.2), channel_id=1, source_target_pairs={{0,1},{1,0},{2,3},{3,2},{4,5},{5,4},{6,7},{7,6},{8,9},{9,8},{10,11... | collective-permute-start | bytes 393224 | tf_op jit(solution)/shard_map/ppermute | solution.py:59
  183.3 62.6 %all-to-all-start.2 = ((bf16[16,32,16,128]{3,2,1,0:T(8,128)(2,1)}), bf16[16,32,16,128]{3,2,1,0:T(8,128)(2,1)S(1)}, u32[]{:S(2)}, u32[]{:S(2)}) async-start(bf16[16,32,16,128]{3,2,1,0:T(8,128)(2,1)} %broadcast_in_dim.5), calls=%async_computation.2 | async-start | bytes 4194304 | tf_op jit(solution)/shard_map/all_to_all | solution.py:43
Sparse Core Ops, SparseCore 0:
  181.7 51.8 all-gather.1
